TPU v7x, 512 devices: a whole 4x4x16 slice. The times are simulated.
512 devices in a mesh: tm: 16 (over z_hi, y), space: 32 (over z_lo, x, core).
Axes of the slice: x: 4, y: 4, z: 16 (z_hi: 4, z_lo: 4; z = z_hi * 4 + z_lo), core: 2. Of those that a mesh axis runs over, the one named last changes fastest.
Arguments:
- queries: bfloat16 [128, 2048, 256], P('tm', 'space'), as said below
- keys: bfloat16 [128, 2048, 256], P('tm', 'space'), as said below
- label_values: bfloat16 [128, 2048, 64], P('tm', 'space'), may hold values from -6 to 6
- class_ids: int32 [128, 2048], P(None, 'space'), may hold values from 0 to 63
- valid_pixels: int32 [128], replicated, may hold values from 1024 to 2048
- keyframe_index: int32 [2, 2], replicated, may hold values from 0 to 127, as said below
Outputs:
- readout: bfloat16 [128, 2048, 64], P('tm', 'space')
- confidence: float32 [2, 2, 2048], P(None, None, 'space')
Inputs may be any that keep to these rules, and one draw needn't show every extreme that they name: `queries`: queries and keys are real-valued embeddings. `keys`: Real-valued embeddings. `keyframe_index`: all 4 entries are different frames.
All inputs are finite; a program needn't handle non-finite values.
Results may differ from a plain program's by a relative error of at most 0.0053.
Values may be sent and summed in bfloat16 or wider, within the bound.
No kernel may reach another device: no remote copies, remote signals or barrier semaphores. Data moves between devices by JAX's collectives and lax.ppermute only.
A program may use at most 192 MiB of HBM per device.

v0:
```python
import math
import jax
import jax.numpy as jnp
from jax import lax
from jax.sharding import PartitionSpec as P


def from_root(value, axis, root):
    mine = lax.axis_index(axis) == root
    return lax.psum(jnp.where(mine, value, jnp.zeros_like(value)), axis)


def body(queries, keys, label_values, class_ids, valid_pixels, keyframe_index):
    fr_dev, pix_dev, width = queries.shape
    channels = label_values.shape[2]
    total_steps, keyframes = keyframe_index.shape
    pix_all = pix_dev * lax.axis_size("space")
    mem_width = keyframes * pix_all
    time_pos = lax.axis_index("tm")
    space_pos = lax.axis_index("space")
    rows = fr_dev * pix_dev
    block_rows = 512
    blocks = rows // block_rows
    frame_valid = lax.dynamic_slice_in_dim(valid_pixels, time_pos * fr_dev, fr_dev)
    pixel_ids = space_pos * pix_dev + jnp.arange(pix_dev, dtype=jnp.int32)
    row_valid = (pixel_ids[None, :] < frame_valid[:, None]).reshape(blocks, block_rows)
    query_blocks = queries.reshape(blocks, block_rows, width)
    scale = 3.0 / math.sqrt(width)
    class_range = jnp.arange(channels, dtype=jnp.int32)
    current = label_values
    confidences = []
    readout = label_values
    for step in range(total_steps):
        chosen = keyframe_index[step]
        owners = chosen // fr_dev
        slots = chosen % fr_dev
        local_keys = jnp.take(keys, slots, axis=0)
        local_values = jnp.take(current, slots, axis=0)
        joined = jnp.concatenate([local_keys, local_values], axis=2)
        fetched = []
        for number in range(keyframes):
            fetched.append(from_root(joined[number], "tm", owners[number]))
        fetched = jnp.stack(fetched)
        part_keys = fetched[:, :, :width]
        part_values = fetched[:, :, width:]
        part_ids = jnp.take(class_ids, chosen, axis=0).astype(jnp.bfloat16)
        mem_keys, mem_values, mem_ids = (
            lax.all_gather(part_keys, "space", axis=1, tiled=True),
            lax.all_gather(part_values, "space", axis=1, tiled=True),
            lax.all_gather(part_ids, "space", axis=1, tiled=True),
        )
        mem_keys = mem_keys.reshape(mem_width, width)
        mem_values = mem_values.reshape(mem_width, channels)
        mem_ids = mem_ids.reshape(mem_width).astype(jnp.int32)
        key_valid = (
            jnp.arange(pix_all, dtype=jnp.int32)[None, :] < jnp.take(valid_pixels, chosen)[:, None]
        ).reshape(mem_width)
        class_match = mem_ids[None, :] == class_range[:, None]
        onehot_t = class_match.astype(jnp.bfloat16)

        def score_block(query_rows):
            raw = lax.dot_general(
                query_rows, mem_keys, (((1,), (1,)), ((), ())), preferred_element_type=jnp.float32
            )
            return raw * scale

        def forward(scores, valid_rows):
            masked = jnp.where(key_valid[None, :], scores, -1e30)
            row_max = jnp.max(masked, axis=1, keepdims=True)
            weights = jnp.where(key_valid[None, :], jnp.exp(scores - row_max), 0.0)
            total = jnp.sum(weights, axis=1, keepdims=True)
            mixed = (
                jnp.dot(
                    weights.astype(jnp.bfloat16), mem_values, preferred_element_type=jnp.float32
                )
                / total
            )
            return jnp.where(valid_rows[:, None], mixed, 0.0).astype(jnp.bfloat16)

        lowest = jnp.full((mem_width,), -1e30, jnp.float32)
        zeros_col = jnp.zeros((mem_width,), jnp.float32)

        def first_pass(col_max, inputs):
            query_rows, valid_rows = inputs
            scores = score_block(query_rows)
            block_out = forward(scores, valid_rows)
            local_max = jnp.max(jnp.where(valid_rows[:, None], scores, -1e30), axis=0)
            return (jnp.maximum(col_max, local_max), block_out)

        col_max, out_blocks = lax.scan(first_pass, lowest, (query_blocks, row_valid))
        col_max = lax.pmax(col_max, ("tm", "space"))

        def second_pass(carry, inputs):
            query_rows, valid_rows, block_out = inputs
            scores = score_block(query_rows)
            expo = jnp.where(valid_rows[:, None], jnp.exp(scores - col_max[None, :]), 0.0)
            picked = jnp.dot(block_out, onehot_t, preferred_element_type=jnp.float32)
            return (
                (carry[0] + jnp.sum(expo, axis=0), carry[1] + jnp.sum(expo * picked, axis=0)),
                None,
            )

        (col_total, col_num), unused = lax.scan(
            second_pass, (zeros_col, zeros_col), (query_blocks, row_valid, out_blocks)
        )
        col_total, col_num = lax.psum((col_total, col_num), ("tm", "space"))
        readout = out_blocks.reshape(fr_dev, pix_dev, channels)
        hits = (class_match & key_valid[None, :]).astype(jnp.int32)
        counts = jnp.sum(hits, axis=1)
        all_count = jnp.sum(counts)
        own = jnp.sum(jnp.where(class_match, counts[:, None], 0), axis=0)
        own_safe = jnp.where(key_valid, own, 1)
        factor = jnp.sqrt(all_count.astype(jnp.float32) / (channels * own_safe.astype(jnp.float32)))
        conf_full = jnp.where(key_valid, col_num / col_total * factor, 0.0).reshape(
            keyframes, pix_all
        )
        confidences.append(lax.dynamic_slice_in_dim(conf_full, space_pos * pix_dev, pix_dev, 1))
        current = readout
    return (readout, jnp.stack(confidences))


def solution(mesh):
    placed = (
        P("tm", "space", None),
        P("tm", "space", None),
        P("tm", "space", None),
        P(None, "space"),
        P(),
        P(),
    )
    return jax.shard_map(
        body,
        mesh=mesh,
        in_specs=placed,
        out_specs=(P("tm", "space", None), P(None, None, "space")),
        check_vma=False,
    )
```

profile of v0, /device:TPU:1, one launch (start us, length us, event | category | flops | bytes accessed | tf_op | source)
XLA Modules:
  0.0 1291.4 jit_solution(1095203512651782425)
XLA Ops:
  7.2 0.8 and_select_fusion.1
  8.0 1.5 gather_fusion.3
  9.5 1.5 gather_fusion.4
  11.0 0.1 broadcast_select_fusion
  11.1 0.1 broadcast_select_fusion.3
  11.2 0.7 fusion.46
  13.2 0.7 fusion.41
  13.9 0.0 all-gather.5.cloned.1.call-start
  13.9 188.7 %all-reduce.11.cloned.1.call-done = (bf16[1,64,320]{2,1,0:T(8,128)(2,1)}, bf16[1,64,320]{2,1,0:T(8,128)(2,1)}) async-done(((bf16[1,64,320]{2,1,0:T(8,128)(2,1)}, bf16[1,64,320]{2,1,0:T(8,128)(2,1)}), (bf16[1,64,320]{2,1,0:T(8,128)(2,1)}, bf16[1,64,320]{2,1,0:T(8,128)(2,1)})) %all-reduce.11.cloned.1.call-update) | async-done | bytes 81936 | tf_op jit(solution)/shard_map/psum | solution.py:10
  202.6 0.8 constant_dynamic-update-slice_fusion.1
  203.4 0.8 constant_dynamic-update-slice_fusion
  204.2 0.6 slice.74
  205.0 0.7 dynamic_slice.32
  205.7 0.1 broadcast_compare_fusion
  205.8 0.1 lt.99
  205.9 0.8 compare_and_fusion.3
  206.6 1.3 gather_fusion.2
  207.9 1.3 gather_fusion
  209.2 0.1 iota_compare_fusion.4
  209.4 1.5 gather_fusion.1
  212.2 0.1 broadcast_select_fusion.1
  212.3 56.8 %all_gather.19 = bf16[2,2048,64]{2,1,0:T(8,128)(2,1)S(1)} all-gather(bf16[2,64,64]{2,1,0:T(8,128)(2,1)S(1)} %slice.75), channel_id=1, replica_groups=mesh['tm'=16,'space'=32] {'space'}, dimensions={1}, use_global_device_ids=true | all-gather | bytes 540672 | tf_op jit(solution)/shard_map/all_gather | solution.py:49
  269.1 13.7 %all-gather.5.cloned.1.call-done = bf16[2,2048,256]{2,1,0:T(8,128)(2,1)} async-done(((bf16[2,64,256]{2,1,0:T(8,128)(2,1)}), bf16[2,2048,256]{2,1,0:T(8,128)(2,1)}) %all-gather.5.cloned.1.call-update) | async-done | bytes 2097168 | tf_op jit(solution)/shard_map/all_gather | solution.py:48
  282.8 6.0 select_reduce_fusion.1
  288.9 104.7 %pmax.14 = f32[4096]{0:T(1024)S(1)} all-reduce(f32[4096]{0:T(1024)S(1)} %broadcast_maximum_fusion.1), channel_id=1, replica_groups=mesh['tm'=16,'space'=32] {'tm','space'}, use_global_device_ids=true, to_apply=%region_9.13 | all-reduce | flops 4096 | bytes 32768 | tf_op jit(solution)/shard_map/pmax | solution.py:91
  393.5 7.0 fusion.6
  400.6 1.5 fusion.20
  402.1 0.1 copy.35
  402.2 0.6 gather_fusion.5
  402.8 0.1 broadcast_select_fusion.2
  402.9 0.7 fusion.40
  403.5 0.0 all-gather.7.cloned.1.call-start
  403.6 176.6 %all-reduce.9.cloned.1.call-done = (bf16[1,64,320]{2,1,0:T(8,128)(2,1)}, bf16[1,64,320]{2,1,0:T(8,128)(2,1)}) async-done(((bf16[1,64,320]{2,1,0:T(8,128)(2,1)}, bf16[1,64,320]{2,1,0:T(8,128)(2,1)}), (bf16[1,64,320]{2,1,0:T(8,128)(2,1)}, bf16[1,64,320]{2,1,0:T(8,128)(2,1)})) %all-reduce.9.cloned.1.call-update) | async-done | bytes 81936 | tf_op jit(solution)/shard_map/psum | solution.py:10
  580.2 0.8 constant_dynamic-update-slice_fusion.3
  581.0 0.8 constant_dynamic-update-slice_fusion.2
  581.8 0.6 slice.78
  582.5 0.1 copy.30
  582.6 0.6 gather_fusion.6
  583.1 0.6 gather_fusion.7
  583.7 0.1 fusion.42
  583.8 53.1 %all-gather = bf16[32,64,2]{1,2,0:T(2,128)(2,1)S(1)} all-gather(bf16[1,64,2]{1,2,0:T(2,128)(2,1)S(1)} %fusion.42), channel_id=1, replica_groups=mesh['tm'=16,'space'=32] {'space'}, dimensions={0}, use_global_device_ids=true | all-gather | bytes 8448 | tf_op jit(solution)/shard_map/all_gather | solution.py:50
  636.9 0.1 reshape.240
  637.0 0.1 iota_compare_fusion.5
  637.1 0.1 fusion.43
  637.2 37.6 %all-gather.1 = bf16[32,64,2]{1,2,0:T(2,128)(2,1)S(1)} all-gather(bf16[1,64,2]{1,2,0:T(2,128)(2,1)S(1)} %fusion.43), channel_id=1, replica_groups=mesh['tm'=16,'space'=32] {'space'}, dimensions={0}, use_global_device_ids=true | all-gather | bytes 8448 | tf_op jit(solution)/shard_map/all_gather | solution.py:50
  674.8 0.1 reshape.241
  674.9 1.1 convert_reduce_fusion.3
  676.0 1.0 convert_reduce_fusion.1
  677.0 0.2 select_reduce_fusion.5
  677.2 5.3 fusion.1
  682.5 42.2 %all_gather.21 = bf16[2,2048,64]{2,1,0:T(8,128)(2,1)S(1)} all-gather(bf16[2,64,64]{2,1,0:T(8,128)(2,1)S(1)} %slice.79), channel_id=1, replica_groups=mesh['tm'=16,'space'=32] {'space'}, dimensions={1}, use_global_device_ids=true | all-gather | bytes 540672 | tf_op jit(solution)/shard_map/all_gather | solution.py:49
  724.7 6.0 select_reduce_fusion
  730.7 101.4 %pmax.15 = f32[4096]{0:T(1024)S(1)} all-reduce(f32[4096]{0:T(1024)S(1)} %broadcast_maximum_fusion), channel_id=1, replica_groups=mesh['tm'=16,'space'=32] {'tm','space'}, use_global_device_ids=true, to_apply=%region_18.23 | all-reduce | flops 4096 | bytes 32768 | tf_op jit(solution)/shard_map/pmax | solution.py:91
  832.1 7.0 fusion.7
  839.1 1.5 fusion.29
  840.6 3.2 fusion
  843.9 0.2 select_reduce_fusion.4
  845.4 0.8 copy.36
  846.2 436.3 %all-reduce.7.cloned.1.call-done = (f32[4096]{0:T(1024)}, f32[4096]{0:T(1024)}, f32[4096]{0:T(1024)}, f32[4096]{0:T(1024)}) async-done(((f32[4096]{0:T(1024)}, f32[4096]{0:T(1024)}, f32[4096]{0:T(1024)}, f32[4096]{0:T(1024)}), (f32[4096]{0:T(1024)}, f32[4096]{0:T(1024)}, f32[4096]{0:T(1024)}, f32[4096]{0:T(1024)})) %all-reduce.7.cloned.1.call-update) | async-done | bytes 65552 | tf_op jit(solution)/shard_map/psum | solution.py:106
  1282.5 0.8 multiply_select_fusion.1
  1283.3 0.8 multiply_select_fusion
  1284.1 0.1 dynamic-slice_bitcast_fusion.1
  1284.2 0.1 dynamic-slice_bitcast_fusion
  1284.3 0.6 pad_maximum_fusion.2
  (36 shorter events, 0.4 us)
Async XLA Ops:
  7.2 275.7 %copy-start = (bf16[8,64,256]{2,1,0:T(8,128)(2,1)S(1)}, bf16[8,64,256]{2,1,0:T(8,128)(2,1)}, u32[]{:S(2)}) copy-start(bf16[8,64,256]{2,1,0:T(8,128)(2,1)} %param.14) | copy-start | bytes 786436
  7.2 195.5 %all-reduce.11.cloned.1.call-start = ((), (), s32[]{:S(2)}) async-start(), calls=%async_computation.4 | async-start | bytes 196608 | tf_op jit(solution)/shard_map/psum | solution.py:10
  13.9 269.0 %all-gather.5.cloned.1.call-start = ((), (), s32[]{:S(2)}) async-start(), calls=%async_computation | async-start | bytes 2162688 | tf_op jit(solution)/shard_map/all_gather | solution.py:48
  204.9 375.2 %all-reduce.9.cloned.1.call-start = ((), (), s32[]{:S(2)}) async-start(), calls=%async_computation.3 | async-start | bytes 196608 | tf_op jit(solution)/shard_map/psum | solution.py:10
  393.5 7.0 copy-start.1
  393.5 188.9 %copy-start.3 = (s32[128,64]{0,1:T(8,128)S(1)}, s32[128,64]{0,1:T(8,128)}, u32[]{:S(2)}) copy-start(s32[128,64]{0,1:T(8,128)} %param.17) | copy-start | bytes 98308
  403.5 321.1 %all-gather.7.cloned.1.call-start = ((), (), s32[]{:S(2)}) async-start(), calls=%async_computation.1 | async-start | bytes 2162688 | tf_op jit(solution)/shard_map/all_gather | solution.py:48
  582.4 700.1 %all-reduce.7.cloned.1.call-start = ((), (), s32[]{:S(2)}) async-start(), calls=%async_computation.2 | async-start | bytes 131072 | tf_op jit(solution)/shard_map/psum | solution.py:106
  832.1 7.0 copy-start.2
Sparse Core Ops, SparseCore 0:
  14.0 188.6 all-reduce.10
  205.6 77.1 all-gather.4
  403.7 176.4 all-reduce.8
  582.7 77.0 all-gather.6
  844.0 438.5 all-reduce.6
where the time goes:
time: 1290 us
  waiting for transfers between devices  815 us (63%)
  blocking collectives  396 us (31%)
  matrix products  23.6 us (2%)
  other arithmetic  22.3 us (2%)
  between operations  17.9 us (1%)
  local copies, waits for them, and re-layouts  16.1 us (1%)
    psum x1, waiting for transfers between devices, body(): col_total, col_num = lax.psum((col_total, col_num), ('tm', 'space'))  436 us
    psum x2, waiting for transfers between devices, from_root(): return lax.psum(jnp.where(mine, value, jnp.zeros_like(value)), axis)  365 us
    pmax x2, blocking collectives, body(): col_max = lax.pmax(col_max, ('tm', 'space'))  206 us
    all_gather x2, blocking collectives, body(): lax.all_gather(part_values, 'space', axis=1, tiled=True)  99 us
    all_gather x2, blocking collectives, body(): lax.all_gather(part_ids, 'space', axis=1, tiled=True)  90.7 us
  transfers between devices with their start and end apart: 5, of which 4 were waited for; matrix products, arithmetic and copies ran while one was open for 1% of the time, Pallas kernels for 0%

commit v1 on v0

--- a/solution.py
+++ b/solution.py
@@ -7,7 +7,7 @@
 
 def from_root(value, axis, root):
     mine = lax.axis_index(axis) == root
-    return lax.psum(jnp.where(mine, value, jnp.zeros_like(value)), axis)
+    return jnp.sum(lax.all_gather(jnp.where(mine, value, jnp.zeros_like(value)), axis), axis=0)
 
 
 def body(queries, keys, label_values, class_ids, valid_pixels, keyframe_index):

time: 1290 us -> 1130 us (0.88)
  waiting for transfers between devices: 815 us -> 440 us
  blocking collectives: 396 us -> 617 us
    psum x2 -> x0, waiting for transfers between devices: 365 us -> none  [from_root(): return lax.psum(jnp.where(mine, value, jnp.zeros_like(value)), axis)]
    all_gather x0 -> x4, blocking collectives: none -> 216 us  [from_root(): lax.all_gather(jnp.where(mine, value, jnp.zeros_like(value)), axis)]
  transfers between devices with their start and end apart: 5 -> 3, of which waited for: 4 -> 2; matrix products, arithmetic and copies ran while one was open for 1% -> 1% of each run, Pallas kernels for 0% -> 0%
where the time goes in v1:
time: 1130 us
  blocking collectives  617 us (55%)
  waiting for transfers between devices  440 us (39%)
  matrix products  23.6 us (2%)
  other arithmetic  22.8 us (2%)
  between operations  17.8 us (2%)
  local copies, waits for them, and re-layouts  11.6 us (1%)
    psum x1, waiting for transfers between devices, body(): col_total, col_num = lax.psum((col_total, col_num), ('tm', 'space'))  436 us
    all_gather x4, blocking collectives, from_root(): lax.all_gather(jnp.where(mine, value, jnp.zeros_like(value)), axis)  216 us
    pmax x2, blocking collectives, body(): col_max = lax.pmax(col_max, ('tm', 'space'))  204 us
    all_gather x2, blocking collectives, body(): lax.all_gather(part_values, 'space', axis=1, tiled=True)  108 us
    all_gather x2, blocking collectives, body(): lax.all_gather(part_ids, 'space', axis=1, tiled=True)  88.3 us
  transfers between devices with their start and end apart: 3, of which 2 were waited for; matrix products, arithmetic and copies ran while one was open for 1% of the time, Pallas kernels for 0%

profile of v1, /device:TPU:1, one launch (start us, length us, event | category | flops | bytes accessed | tf_op | source)
XLA Modules:
  0.0 1133.1 jit_solution(5651233344326770821)
XLA Ops:
  7.2 0.8 and_select_fusion.3
  8.0 1.5 gather_fusion.3
  9.5 1.5 gather_fusion.4
  11.0 0.1 broadcast_select_fusion
  11.1 0.1 broadcast_select_fusion.3
  11.2 0.7 fusion.48
  13.1 62.1 %all_gather.34 = bf16[16,64,320]{2,1,0:T(8,128)(2,1)S(1)} all-gather(bf16[1,64,320]{2,1,0:T(8,128)(2,1)S(1)} %get-tuple-element.148), channel_id=1, replica_groups=mesh['tm'=16,'space'=32] {'tm'}, dimensions={0}, use_global_device_ids=true | all-gather | bytes 696320 | tf_op jit(solution)/shard_map/all_gather | solution.py:10
  75.2 46.3 %all_gather.35 = bf16[16,64,320]{2,1,0:T(8,128)(2,1)S(1)} all-gather(bf16[1,64,320]{2,1,0:T(8,128)(2,1)S(1)} %get-tuple-element.149), channel_id=1, replica_groups=mesh['tm'=16,'space'=32] {'tm'}, dimensions={0}, use_global_device_ids=true | all-gather | bytes 696320 | tf_op jit(solution)/shard_map/all_gather | solution.py:10
  121.5 0.1 reduce_sum.162
  121.6 0.1 reduce_sum.163
  121.8 0.6 fusion.37
  122.4 0.0 all-gather.7.cloned.1.call-start
  122.5 0.7 dynamic_slice.32
  123.2 0.1 broadcast_compare_fusion
  123.3 0.1 lt.99
  123.4 0.8 compare_and_fusion.3
  124.2 1.3 gather_fusion.2
  125.5 1.3 gather_fusion
  126.8 0.1 iota_compare_fusion.4
  126.9 1.5 gather_fusion.1
  129.7 0.1 broadcast_select_fusion.1
  129.8 67.0 %all_gather.37 = bf16[2,2048,64]{2,1,0:T(8,128)(2,1)S(1)} all-gather(bf16[2,64,64]{2,1,0:T(8,128)(2,1)S(1)} %pad_maximum_fusion.3), channel_id=1, replica_groups=mesh['tm'=16,'space'=32] {'space'}, dimensions={1}, use_global_device_ids=true | all-gather | bytes 540672 | tf_op jit(solution)/shard_map/all_gather | solution.py:49
  196.9 4.7 all-gather.5.cloned.1.call-done
  201.6 6.0 select_reduce_fusion.1
  207.6 104.2 %pmax.14 = f32[4096]{0:T(1024)S(1)} all-reduce(f32[4096]{0:T(1024)S(1)} %broadcast_maximum_fusion.1), channel_id=1, replica_groups=mesh['tm'=16,'space'=32] {'tm','space'}, use_global_device_ids=true, to_apply=%region_9.13 | all-reduce | flops 4096 | bytes 32768 | tf_op jit(solution)/shard_map/pmax | solution.py:91
  311.9 7.0 fusion.6
  318.9 1.5 fusion.20
  320.4 0.1 copy.35
  320.5 0.6 gather_fusion.5
  321.1 0.1 broadcast_select_fusion.2
  321.2 57.3 %all_gather.38 = bf16[16,64,320]{2,1,0:T(8,128)(2,1)S(1)} all-gather(bf16[1,64,320]{2,1,0:T(8,128)(2,1)S(1)} %get-tuple-element.146), channel_id=1, replica_groups=mesh['tm'=16,'space'=32] {'tm'}, dimensions={0}, use_global_device_ids=true | all-gather | bytes 696320 | tf_op jit(solution)/shard_map/all_gather | solution.py:10
  378.5 0.1 reduce_sum.165
  378.7 50.3 %all_gather.39 = bf16[16,64,320]{2,1,0:T(8,128)(2,1)S(1)} all-gather(bf16[1,64,320]{2,1,0:T(8,128)(2,1)S(1)} %get-tuple-element.147), channel_id=1, replica_groups=mesh['tm'=16,'space'=32] {'tm'}, dimensions={0}, use_global_device_ids=true | all-gather | bytes 696320 | tf_op jit(solution)/shard_map/all_gather | solution.py:10
  428.9 0.1 reduce_sum.166
  429.1 0.6 fusion.36
  429.7 0.0 all-reduce.3.cloned.1.call-start
  429.8 0.1 copy.30
  429.9 0.6 gather_fusion.6
  430.5 0.6 gather_fusion.7
  431.0 0.1 fusion.44
  431.1 49.0 %all-gather = bf16[32,64,2]{1,2,0:T(2,128)(2,1)S(1)} all-gather(bf16[1,64,2]{1,2,0:T(2,128)(2,1)S(1)} %fusion.44), channel_id=1, replica_groups=mesh['tm'=16,'space'=32] {'space'}, dimensions={0}, use_global_device_ids=true | all-gather | bytes 8448 | tf_op jit(solution)/shard_map/all_gather | solution.py:50
  480.1 0.1 reshape.224
  480.2 0.1 iota_compare_fusion.5
  480.3 0.1 fusion.45
  480.4 39.3 %all-gather.1 = bf16[32,64,2]{1,2,0:T(2,128)(2,1)S(1)} all-gather(bf16[1,64,2]{1,2,0:T(2,128)(2,1)S(1)} %fusion.45), channel_id=1, replica_groups=mesh['tm'=16,'space'=32] {'space'}, dimensions={0}, use_global_device_ids=true | all-gather | bytes 8448 | tf_op jit(solution)/shard_map/all_gather | solution.py:50
  519.7 0.1 reshape.225
  519.8 1.1 convert_reduce_fusion.3
  520.9 1.0 convert_reduce_fusion.1
  521.9 0.2 select_reduce_fusion.5
  522.1 40.9 %all_gather.41 = bf16[2,2048,64]{2,1,0:T(8,128)(2,1)S(1)} all-gather(bf16[2,64,64]{2,1,0:T(8,128)(2,1)S(1)} %pad_maximum_fusion.2), channel_id=1, replica_groups=mesh['tm'=16,'space'=32] {'space'}, dimensions={1}, use_global_device_ids=true | all-gather | bytes 540672 | tf_op jit(solution)/shard_map/all_gather | solution.py:49
  563.1 5.3 fusion.1
  568.3 6.0 select_reduce_fusion
  574.4 100.0 %pmax.15 = f32[4096]{0:T(1024)S(1)} all-reduce(f32[4096]{0:T(1024)S(1)} %broadcast_maximum_fusion), channel_id=1, replica_groups=mesh['tm'=16,'space'=32] {'tm','space'}, use_global_device_ids=true, to_apply=%region_18.23 | all-reduce | flops 4096 | bytes 32768 | tf_op jit(solution)/shard_map/pmax | solution.py:91
  674.4 7.0 fusion.7
  681.5 1.5 fusion.29
  683.0 3.2 fusion
  686.2 0.2 select_reduce_fusion.4
  687.8 0.8 copy.36
  688.5 435.7 %all-reduce.3.cloned.1.call-done = (f32[4096]{0:T(1024)}, f32[4096]{0:T(1024)}, f32[4096]{0:T(1024)}, f32[4096]{0:T(1024)}) async-done(((f32[4096]{0:T(1024)}, f32[4096]{0:T(1024)}, f32[4096]{0:T(1024)}, f32[4096]{0:T(1024)}), (f32[4096]{0:T(1024)}, f32[4096]{0:T(1024)}, f32[4096]{0:T(1024)}, f32[4096]{0:T(1024)})) %all-reduce.3.cloned.1.call-update) | async-done | bytes 65552 | tf_op jit(solution)/shard_map/psum | solution.py:106
  1124.3 0.8 multiply_select_fusion.1
  1125.0 0.8 multiply_select_fusion
  1125.8 0.1 dynamic-slice_bitcast_fusion.1
  1125.9 0.1 dynamic-slice_bitcast_fusion
  1126.0 0.6 pad_maximum_fusion.4
  (34 shorter events, 0.3 us)
Async XLA Ops:
  7.2 194.4 %copy-start = (bf16[8,64,256]{2,1,0:T(8,128)(2,1)S(1)}, bf16[8,64,256]{2,1,0:T(8,128)(2,1)}, u32[]{:S(2)}) copy-start(bf16[8,64,256]{2,1,0:T(8,128)(2,1)} %param.14) | copy-start | bytes 786436
  7.2 194.4 %all-gather.5.cloned.1.call-start = ((), (), s32[]{:S(2)}) async-start(), calls=%async_computation | async-start | bytes 2162688 | tf_op jit(solution)/shard_map/all_gather | solution.py:48
  122.4 445.9 %all-gather.7.cloned.1.call-start = ((), (), s32[]{:S(2)}) async-start(), calls=%async_computation.1 | async-start | bytes 2162688 | tf_op jit(solution)/shard_map/all_gather | solution.py:48
  311.9 7.0 copy-start.1
  318.9 110.9 %copy-start.3 = (s32[128,64]{0,1:T(8,128)S(1)}, s32[128,64]{0,1:T(8,128)}, u32[]{:S(2)}) copy-start(s32[128,64]{0,1:T(8,128)} %param.17) | copy-start | bytes 98308
  429.7 694.5 %all-reduce.3.cloned.1.call-start = ((), (), s32[]{:S(2)}) async-start(), calls=%async_computation.2 | async-start | bytes 131072 | tf_op jit(solution)/shard_map/psum | solution.py:106
  674.4 7.0 copy-start.2
Sparse Core Ops, SparseCore 0:
  122.6 78.9 all-gather.4
  429.9 70.8 all-gather.6
  686.3 437.8 all-reduce.2
